TPU v7x, 32 devices: a whole 2x2x4 slice. The times are simulated.
32 devices in a mesh: fsdp: 4 (over y, x), seq: 8 (over z, core).
Axes of the slice: x: 2, y: 2, z: 4, core: 2. Of those that a mesh axis runs over, the one named last changes fastest.
Arguments:
- events: bfloat16 [4, 1024, 2048], P('fsdp', 'seq'), may hold values from -6 to 6
- type_ids: int32 [4, 1024], P('fsdp', 'seq'), may hold values from 0 to 255
- type_table: bfloat16 [256, 2048], P('fsdp'), may hold values from -6 to 6
- norm_gain: float32 [2048], replicated, may hold values from 0.25 to 1.75
- kernel: bfloat16 [2048, 1152], P('fsdp'), may hold values from -0.1875 to 0.1875
- upstream: bfloat16 [4, 1024, 2048], P('fsdp', 'seq'), may hold values from -6 to 6
Outputs:
- input_grad: bfloat16 [4, 1024, 2048], P('fsdp', 'seq')
- table_grad: float32 [256, 2048], P(('fsdp', 'seq'))
- gain_grad: float32 [2048], P(('fsdp', 'seq'))
- kernel_grad: float32 [2048, 1152], P('seq')
All inputs are finite; a program needn't handle non-finite values.
Results may differ from a plain program's by a relative error of at most 0.0053.
Values may be sent and summed in bfloat16 or wider, within the bound.
No kernel may reach another device: no remote copies, remote signals or barrier semaphores. Data moves between devices by JAX's collectives and lax.ppermute only.
A program may use at most 128 MiB of HBM per device.

v0:
```python
import jax
import jax.numpy as jnp
from jax import lax
from jax.sharding import PartitionSpec as P

GROUPS = 16
KERNEL = 9


def with_halo(cells, axis, dim, width):
    count = lax.axis_size(axis)
    ends = count - 1
    head = lax.slice_in_dim(cells, 0, width, axis=dim)
    tail = lax.slice_in_dim(cells, cells.shape[dim] - width, cells.shape[dim], axis=dim)
    return jnp.concatenate(
        [
            lax.ppermute(tail, axis, [(i, (i + 1) % count) for i in range(ends)]),
            cells,
            lax.ppermute(head, axis, [((i + 1) % count, i) for i in range(ends)]),
        ],
        axis=dim,
    )


def from_partner(value, axis, apart):
    mask = 2**apart
    pairs = [(source, source ^ mask) for source in range(lax.axis_size(axis))]
    return lax.ppermute(value, axis, pairs)


def gather_rows(block, axis):
    count = lax.axis_size(axis)
    return lax.all_to_all(
        jnp.tile(block, (count,) + (1,) * (block.ndim - 1)), axis, 0, 0, tiled=True
    )


def conv_forward(padded, weights, length):
    chans = padded.shape[-1]
    total = None
    for k in range(KERNEL):
        term = jnp.einsum(
            "gtc,goc->gto",
            padded[:, k : k + length],
            weights[:, :, k * chans : (k + 1) * chans],
            preferred_element_type=jnp.float32,
        )
        total = term if total is None else total + term
    return total


def conv_backward(dpad, weights, length):
    chans = weights.shape[-1] // KERNEL
    half = KERNEL // 2
    total = None
    for k in range(KERNEL):
        term = jnp.einsum(
            "gto,goc->gtc",
            dpad[:, 2 * half - k : 2 * half - k + length],
            weights[:, :, k * chans : (k + 1) * chans],
            preferred_element_type=jnp.float32,
        )
        total = term if total is None else total + term
    return total


def spread_groups(normed, dflat, chans):
    normed_slice = lax.all_to_all(normed, "seq", 1, 0, tiled=True)
    dconv_slice = lax.all_to_all(dflat, "seq", 1, 0, tiled=True)
    whole, slice_width = normed_slice.shape
    spread = chans // slice_width
    position = lax.axis_index("seq")
    group_rows = normed_slice
    for bit in range(spread.bit_length() - 1):
        partner = from_partner(group_rows, "seq", bit)
        lower = position >> bit & 1 == 0
        group_rows = jnp.where(
            lower,
            jnp.concatenate([group_rows, partner], axis=1),
            jnp.concatenate([partner, group_rows], axis=1),
        )
    return (group_rows.reshape(1, whole, chans), dconv_slice.reshape(1, whole, slice_width))


def sum_rows(block, axis):
    count = lax.axis_size(axis)
    parts = block.reshape(count, block.shape[0] // count, *block.shape[1:])
    return lax.all_to_all(parts, axis, 0, 0, tiled=True).sum(axis=0)


def psum_rows(block, axis):
    return gather_rows(sum_rows(block, axis), axis)


def table_and_gain(input_grad, ids, gain_term, types, scale):
    every = ("fsdp", "seq")
    count = lax.axis_size("fsdp") * lax.axis_size("seq")
    length, width = input_grad.shape
    narrow = width // count
    id_rows = -(-length // narrow)
    ids_wide = (
        jnp.zeros((id_rows * narrow,), jnp.bfloat16).at[:length].set(ids.astype(jnp.bfloat16))
    )
    send = jnp.concatenate(
        [
            input_grad.reshape(length, count, narrow).transpose(1, 0, 2),
            jnp.broadcast_to(ids_wide.reshape(1, id_rows, narrow), (count, id_rows, narrow)),
        ],
        axis=1,
    )
    got = lax.all_to_all(send, every, 0, 0, tiled=True)
    rows_all = got[:, :length].reshape(count * length, narrow)
    ids_all = (
        got[:, length:].reshape(count, id_rows * narrow)[:, :length].reshape(-1).astype(jnp.int32)
    )
    onehot = (ids_all[:, None] == jnp.arange(types, dtype=jnp.int32)[None, :]).astype(jnp.bfloat16)
    columns = lax.dot_general(
        onehot, rows_all, (((0,), (0,)), ((), ())), preferred_element_type=jnp.float32
    )
    columns = columns * scale
    per = types // count
    back = jnp.concatenate(
        [columns.reshape(count, per, narrow), gain_term.reshape(count, 1, narrow)], axis=1
    )
    back = lax.all_to_all(back, every, 0, 0, tiled=True)
    table_grad = back[:, :per].transpose(1, 0, 2).reshape(per, width)
    gain_grad = back[:, per].sum(axis=0)
    return (table_grad, gain_grad)


def body(events, type_ids, type_table, norm_gain, kernel, upstream):
    length = events.shape[1]
    width = events.shape[2]
    chans = width // GROUPS
    half = KERNEL // 2
    fsdp = lax.axis_size("fsdp")
    seq_count = lax.axis_size("seq")
    total = length * seq_count * fsdp
    scale = 1.0 / jnp.sqrt(jnp.float32(total))
    table = gather_rows(type_table, "fsdp")
    types = table.shape[0]
    onehot = (type_ids[0][:, None] == jnp.arange(types, dtype=jnp.int32)[None, :]).astype(
        jnp.bfloat16
    )
    mixed = events[0].astype(jnp.float32) + jnp.dot(
        onehot, table, preferred_element_type=jnp.float32
    )
    inv = lax.rsqrt(jnp.mean(mixed * mixed, axis=-1, keepdims=True) + 1e-06)
    normed = (mixed * inv * norm_gain).astype(jnp.bfloat16)
    normed_g = normed.reshape(length, GROUPS, chans).transpose(1, 0, 2)
    padded = with_halo(normed_g, "seq", 1, half)
    weights = lax.all_gather(kernel, "fsdp", axis=0, tiled=True).reshape(
        GROUPS, chans, KERNEL * chans
    )
    conv = conv_forward(padded, weights, length)
    up_float = upstream[0].astype(jnp.float32)
    up_g = up_float.reshape(length, GROUPS, chans).transpose(1, 0, 2)
    sig = jax.nn.sigmoid(conv)
    dconv = (up_g * sig * (1.0 + conv * (1.0 - sig))).astype(jnp.bfloat16)
    dpad = with_halo(dconv, "seq", 1, half)
    dnormed = conv_backward(dpad, weights, length)
    if seq_count <= GROUPS:
        group_in = lax.all_to_all(normed_g, "seq", 0, 1, tiled=True)
        group_out = lax.all_to_all(dconv, "seq", 0, 1, tiled=True)
    else:
        group_in, group_out = spread_groups(
            normed, dconv.transpose(1, 0, 2).reshape(length, width), chans
        )
    local_groups = group_in.shape[0]
    whole = group_in.shape[1]
    group_pad = jnp.pad(group_in, ((0, 0), (half, half), (0, 0)))
    kterms = [
        jnp.einsum(
            "gto,gtc->goc",
            group_out,
            group_pad[:, k : k + whole],
            preferred_element_type=jnp.float32,
        )
        for k in range(KERNEL)
    ]
    kernel_part = jnp.concatenate(kterms, axis=-1).reshape(-1, KERNEL * chans) * scale
    dnormed = dnormed.transpose(1, 0, 2).reshape(length, width)
    gain_term = jnp.sum(dnormed * mixed * inv, axis=0) * scale
    scaled = norm_gain * dnormed
    dmixed = inv * scaled - mixed * inv * inv * inv * jnp.mean(
        scaled * mixed, axis=-1, keepdims=True
    )
    input_grad = (up_float + dmixed).astype(jnp.bfloat16)
    kernel_grad = lax.psum(kernel_part, "fsdp")
    table_grad, gain_grad = table_and_gain(input_grad, type_ids[0], gain_term, types, scale)
    return (input_grad[None], table_grad, gain_grad, kernel_grad)


def solution(mesh):
    return jax.shard_map(
        body,
        mesh=mesh,
        in_specs=(
            P("fsdp", "seq", None),
            P("fsdp", "seq"),
            P("fsdp", None),
            P(),
            P("fsdp", None),
            P("fsdp", "seq", None),
        ),
        out_specs=(
            P("fsdp", "seq", None),
            P(("fsdp", "seq"), None),
            P(("fsdp", "seq")),
            P("seq", None),
        ),
        check_vma=False,
    )
```

profile of v0, /device:TPU:0, one launch (start us, length us, event | category | flops | bytes accessed | tf_op | source)
XLA Modules:
  0.0 202.8 jit_solution(586247132597513163)
XLA Ops:
  7.2 0.7 all-gather.2.cloned.1.call-update
  7.9 1.1 tile.2
  9.1 24.3 %all_to_all.55 = bf16[4,64,2048]{2,1,0:T(8,128)(2,1)S(1)} all-to-all(bf16[4,64,2048]{2,1,0:T(8,128)(2,1)S(1)} %tile.2), channel_id=1, replica_groups=mesh['fsdp'=4,'seq'=8] {'fsdp'}, dimensions={0} | all-to-all | bytes 2097152 | tf_op jit(solution)/shard_map/all_to_all | solution.py:33
  33.4 0.4 multiply_reduce_fusion.2
  33.8 1.0 bitcast_bitcast_fusion
  34.8 5.2 %all-to-all-start.4 = ((bf16[16,128,128]{2,1,0:T(8,128)(2,1)}), bf16[16,128,128]{2,1,0:T(8,128)(2,1)S(1)}, u32[]{:S(2)}, u32[]{:S(2)}) async-start(bf16[16,128,128]{2,1,0:T(8,128)(2,1)} %bitcast_bitcast_fusion), calls=%async_computation.4 | async-start | bytes 1048576 | tf_op jit(solution)/shard_map/all_to_all | solution.py:163
  40.1 0.2 copy.126
  40.5 0.8 fusion.148
  41.3 2.4 %collective-permute-start = (bf16[16,4,128]{2,1,0:T(4,128)(2,1)S(1)}, bf16[16,4,128]{2,1,0:T(4,128)(2,1)S(1)}, u32[]{:S(2)}, u32[]{:S(2)}) collective-permute-start(bf16[16,4,128]{2,1,0:T(4,128)(2,1)S(1)} %get-tuple-element.28), channel_id=1, source_target_pairs={{0,1},{1,2},{2,3},{3,4},{4,5},{5,6},{6,7},{8,9},{9,10},{10,11},{11... | collective-permute-start | bytes 49160 | tf_op jit(solution)/shard_map/ppermute | solution.py:17
  43.7 1.3 collective-permute-start.1
  45.0 10.3 %all-to-all-done.4 = bf16[16,128,128]{2,1,0:T(8,128)(2,1)S(1)} async-done(((bf16[16,128,128]{2,1,0:T(8,128)(2,1)}), bf16[16,128,128]{2,1,0:T(8,128)(2,1)S(1)}, u32[]{:S(2)}, u32[]{:S(2)}) %all-to-all-start.4) | async-done | bytes 524320 | tf_op jit(solution)/shard_map/all_to_all | solution.py:163
  55.3 0.3 copy.111
  55.6 1.0 all_to_all.49
  56.7 17.2 %all-gather.2.cloned.1.call-done = bf16[2048,1152]{1,0:T(8,128)(2,1)} async-done(((bf16[512,1152]{1,0:T(8,128)(2,1)}), bf16[2048,1152]{1,0:T(8,128)(2,1)}) %all-gather.2.cloned.1.call-update) | async-done | bytes 4718608 | tf_op jit(solution)/shard_map/all_gather | solution.py:152
  73.8 1.7 fusion.92
  75.6 1.7 fusion.44
  77.2 1.5 fusion.49
  78.8 1.5 fusion.69
  80.3 1.5 fusion.41
  81.8 1.5 fusion.36
  83.4 1.5 fusion.64
  84.9 1.6 fusion.13
  86.5 2.8 %fusion.18 = bf16[16,128,128]{2,1,0:T(8,128)(2,1)} fusion(f32[128,16,128]{2,1,0:T(8,128)S(1)} %bitcast.108, f32[16,128,128]{2,1,0:T(8,128)S(1)} %fusion.64, f32[16,128,128]{2,1,0:T(8,128)S(1)} %fusion.36, f32[16,128,128]{2,1,0:T(8,128)S(1)} %fusion.41, f32[16,128,128]{2,1,0:T(8,128)S(1)} %fusion.13, bf16[16,4,128]{2,1,0:T(4,128)(2,1)S(1)} %collective-permute-done.1, ...), kind=kOutput, calls=%fused_computation.37 | convolution fusion | flops 71565312 | bytes 6832128 | tf_op jit(solution)/shard_map/gtc,goc->gto/dot_general | solution.py:42
  89.3 4.6 %all-to-all-start.3 = ((bf16[16,128,128]{2,1,0:T(8,128)(2,1)}), bf16[16,128,128]{2,1,0:T(8,128)(2,1)}, u32[]{:S(2)}, u32[]{:S(2)}) async-start(bf16[16,128,128]{2,1,0:T(8,128)(2,1)} %fusion.18), calls=%async_computation.3 | async-start | bytes 1048576 | tf_op jit(solution)/shard_map/all_to_all | solution.py:164
  93.9 0.8 fusion.147
  94.8 1.3 collective-permute-start.2
  96.1 1.7 fusion.90
  97.8 3.0 %collective-permute-start.3 = (bf16[16,4,128]{2,1,0:T(4,128)(2,1)S(1)}, bf16[16,4,128]{2,1,0:T(4,128)(2,1)S(1)}, u32[]{:S(2)}, u32[]{:S(2)}) collective-permute-start(bf16[16,4,128]{2,1,0:T(4,128)(2,1)S(1)} %get-tuple-element.27), channel_id=1, source_target_pairs={{0,1},{1,2},{2,3},{3,4},{4,5},{5,6},{6,7},{8,9},{9,10},{10,11},{11... | collective-permute-start | bytes 49160 | tf_op jit(solution)/shard_map/ppermute | solution.py:17
  100.8 1.7 fusion.33
  102.5 1.7 fusion.28
  104.3 1.7 fusion.59
  106.0 1.7 fusion.25
  107.7 1.7 fusion.20
  109.4 1.7 fusion.54
  111.1 1.7 fusion.7
  112.9 1.8 fusion.4
  114.6 0.3 copy.122
  115.0 0.3 multiply_reduce_fusion
  115.3 1.4 fusion.16
  116.7 0.3 copy.102
  117.1 1.3 pad_maximum_fusion
  118.4 9.9 %all-to-all-start.1 = ((bf16[32,130,64]{1,2,0:T(8,128)(2,1)}), bf16[32,130,64]{1,2,0:T(8,128)(2,1)S(1)}, u32[]{:S(2)}, u32[]{:S(2)}) async-start(bf16[32,130,64]{1,2,0:T(8,128)(2,1)} %pad_maximum_fusion), calls=%async_computation.1 | async-start | bytes 2097152 | tf_op jit(solution)/shard_map/all_to_all | solution.py:111
  128.3 0.2 all-reduce.3.cloned.1.call-start
  128.6 1.1 copy.110
  129.6 0.4 convolution_dynamic-update-slice_fusion.8
  130.0 0.4 convolution_dynamic-update-slice_fusion.7
  130.4 0.4 convolution_dynamic-update-slice_fusion.6
  130.7 0.4 convolution_dynamic-update-slice_fusion.5
  131.1 0.3 convolution_dynamic-update-slice_fusion.4
  131.4 0.4 convolution_dynamic-update-slice_fusion.3
  131.8 0.4 convolution_dynamic-update-slice_fusion.2
  132.1 0.4 convolution_dynamic-update-slice_fusion.1
  132.5 0.4 convolution_dynamic-update-slice_fusion
  133.0 1.4 copy.112
  134.5 21.5 %all-to-all-done.1 = bf16[32,130,64]{1,2,0:T(8,128)(2,1)S(1)} async-done(((bf16[32,130,64]{1,2,0:T(8,128)(2,1)}), bf16[32,130,64]{1,2,0:T(8,128)(2,1)S(1)}, u32[]{:S(2)}, u32[]{:S(2)}) %all-to-all-start.1) | async-done | bytes 532512 | tf_op jit(solution)/shard_map/all_to_all | solution.py:111
  156.0 0.3 copy.123
  156.4 0.9 fusion.14
  157.6 9.6 %all_to_all.56 = f32[32,1,576]{2,1,0:T(1,128)S(1)} all-to-all(f32[32,1,576]{2,1,0:T(1,128)S(1)} %reshape.125), channel_id=1, replica_groups=mesh['fsdp'=4,'seq'=8] {'fsdp','seq'}, dimensions={0} | all-to-all | bytes 147456 | tf_op jit(solution)/shard_map/all_to_all | solution.py:125
  167.2 0.5 broadcast.63
  167.7 0.8 reduce.7
  168.7 0.7 reshape.113
  169.4 0.6 slice_reduce_fusion
  170.0 23.7 %all-reduce.3.cloned.1.call-done = f32[256,1152]{1,0:T(8,128)} async-done(((f32[256,1152]{1,0:T(8,128)}), f32[256,1152]{1,0:T(8,128)}) %all-reduce.3.cloned.1.call-update) | async-done | bytes 1179664 | tf_op jit(solution)/shard_map/psum | solution.py:189
  193.6 2.4 %copy.143 = f32[256,1152]{1,0:T(8,128)} copy(f32[256,1152]{1,0:T(8,128)} %all-reduce.3.cloned.1.call-done) | data formatting | bytes 2359296
  (41 shorter events, 1.3 us)
Async XLA Ops:
  7.2 26.2 %copy-start.6 = (s32[1,128]{1,0:T(1,128)S(1)}, s32[1,128]{1,0:T(1,128)}, u32[]{:S(2)}) copy-start(s32[1,128]{1,0:T(1,128)} %param.11) | copy-start | bytes 1540
  7.2 26.2 %copy-start.4 = (bf16[1,128,2048]{2,1,0:T(8,128)(2,1)S(1)}, bf16[1,128,2048]{2,1,0:T(8,128)(2,1)}, u32[]{:S(2)}) copy-start(bf16[1,128,2048]{2,1,0:T(8,128)(2,1)} %param.10) | copy-start | bytes 1572868
  7.2 26.6 %copy-start.5 = (f32[2048]{0:T(1024)S(1)}, f32[2048]{0:T(1024)}, u32[]{:S(2)}) copy-start(f32[2048]{0:T(1024)} %param.13) | copy-start | bytes 24580
  7.2 66.6 %all-gather.2.cloned.1.call-start = ((), (), s32[]{:S(2)}) async-start(), calls=%async_computation.5 | async-start | bytes 5898240 | tf_op jit(solution)/shard_map/all_gather | solution.py:152
  7.9 32.0 %copy-start.1 = (bf16[1,128,2048]{2,1,0:T(8,128)(2,1)S(1)}, bf16[1,128,2048]{2,1,0:T(8,128)(2,1)}, u32[]{:S(2)}) copy-start(bf16[1,128,2048]{2,1,0:T(8,128)(2,1)} %param.15) | copy-start | bytes 1572868
  34.8 20.5 %all-to-all-start.4 = ((bf16[16,128,128]{2,1,0:T(8,128)(2,1)}), bf16[16,128,128]{2,1,0:T(8,128)(2,1)S(1)}, u32[]{:S(2)}, u32[]{:S(2)}) async-start(bf16[16,128,128]{2,1,0:T(8,128)(2,1)} %bitcast_bitcast_fusion), calls=%async_computation.4 | async-start | bytes 1048576 | tf_op jit(solution)/shard_map/all_to_all | solution.py:163
  41.3 34.3 %collective-permute-start = (bf16[16,4,128]{2,1,0:T(4,128)(2,1)S(1)}, bf16[16,4,128]{2,1,0:T(4,128)(2,1)S(1)}, u32[]{:S(2)}, u32[]{:S(2)}) collective-permute-start(bf16[16,4,128]{2,1,0:T(4,128)(2,1)S(1)} %get-tuple-element.28), channel_id=1, source_target_pairs={{0,1},{1,2},{2,3},{3,4},{4,5},{5,6},{6,7},{8,9},{9,10},{10,11},{11... | collective-permute-start | bytes 49160 | tf_op jit(solution)/shard_map/ppermute | solution.py:17
  43.7 36.6 %collective-permute-start.1 = (bf16[16,4,128]{2,1,0:T(4,128)(2,1)S(1)}, bf16[16,4,128]{2,1,0:T(4,128)(2,1)S(1)}, u32[]{:S(2)}, u32[]{:S(2)}) collective-permute-start(bf16[16,4,128]{2,1,0:T(4,128)(2,1)S(1)} %get-tuple-element.29), channel_id=1, source_target_pairs={{1,0},{2,1},{3,2},{4,3},{5,4},{6,5},{7,6},{9,8},{10,9},{11,10},{12... | collective-permute-start | bytes 49160 | tf_op jit(solution)/shard_map/ppermute | solution.py:19
  73.8 3.4 %copy-start = (bf16[2048,1152]{1,0:T(8,128)(2,1)S(1)}, bf16[2048,1152]{1,0:T(8,128)(2,1)}, u32[]{:S(2)}) copy-start(bf16[2048,1152]{1,0:T(8,128)(2,1)} %all-gather.2.cloned.1.call-done) | copy-start | bytes 14155780
  89.3 29.1 %all-to-all-start.3 = ((bf16[16,128,128]{2,1,0:T(8,128)(2,1)}), bf16[16,128,128]{2,1,0:T(8,128)(2,1)}, u32[]{:S(2)}, u32[]{:S(2)}) async-start(bf16[16,128,128]{2,1,0:T(8,128)(2,1)} %fusion.18), calls=%async_computation.3 | async-start | bytes 1048576 | tf_op jit(solution)/shard_map/all_to_all | solution.py:164
  94.8 6.1 %collective-permute-start.2 = (bf16[16,4,128]{2,1,0:T(4,128)(2,1)S(1)}, bf16[16,4,128]{2,1,0:T(4,128)(2,1)S(1)}, u32[]{:S(2)}, u32[]{:S(2)}) collective-permute-start(bf16[16,4,128]{2,1,0:T(4,128)(2,1)S(1)} %get-tuple-element.26), channel_id=1, source_target_pairs={{1,0},{2,1},{3,2},{4,3},{5,4},{6,5},{7,6},{9,8},{10,9},{11,10},{12... | collective-permute-start | bytes 49160 | tf_op jit(solution)/shard_map/ppermute | solution.py:19
  97.8 8.2 %collective-permute-start.3 = (bf16[16,4,128]{2,1,0:T(4,128)(2,1)S(1)}, bf16[16,4,128]{2,1,0:T(4,128)(2,1)S(1)}, u32[]{:S(2)}, u32[]{:S(2)}) collective-permute-start(bf16[16,4,128]{2,1,0:T(4,128)(2,1)S(1)} %get-tuple-element.27), channel_id=1, source_target_pairs={{0,1},{1,2},{2,3},{3,4},{4,5},{5,6},{6,7},{8,9},{9,10},{10,11},{11... | collective-permute-start | bytes 49160 | tf_op jit(solution)/shard_map/ppermute | solution.py:17
  116.7 13.7 %copy-start.3 = (bf16[128,2048]{1,0:T(8,128)(2,1)}, bf16[128,2048]{1,0:T(8,128)(2,1)S(1)}, u32[]{:S(2)}) copy-start(bf16[128,2048]{1,0:T(8,128)(2,1)S(1)} %fusion.16) | copy-start | bytes 1572868
  116.7 12.9 %copy-start.2 = (bf16[2,1024,128]{1,2,0:T(8,128)(2,1)S(1)}, bf16[2,1024,128]{1,2,0:T(8,128)(2,1)}, u32[]{:S(2)}) copy-start(bf16[2,1024,128]{1,2,0:T(8,128)(2,1)} %all_to_all.49) | copy-start | bytes 1572868
  118.4 37.5 %all-to-all-start.1 = ((bf16[32,130,64]{1,2,0:T(8,128)(2,1)}), bf16[32,130,64]{1,2,0:T(8,128)(2,1)S(1)}, u32[]{:S(2)}, u32[]{:S(2)}) async-start(bf16[32,130,64]{1,2,0:T(8,128)(2,1)} %pad_maximum_fusion), calls=%async_computation.1 | async-start | bytes 2097152 | tf_op jit(solution)/shard_map/all_to_all | solution.py:111
  128.3 65.3 %all-reduce.3.cloned.1.call-start = ((), (), s32[]{:S(2)}) async-start(), calls=%async_computation.6 | async-start | bytes 2359296 | tf_op jit(solution)/shard_map/psum | solution.py:189
Sparse Core Ops, SparseCore 0:
  9.9 63.9 all-gather.1
  134.5 59.0 all-reduce.2
where the time goes:
time: 204 us; the launch traced here: 203 us
  waiting for transfers between devices  73.3 us (36%)
  matrix products  35.4 us (17%)
  blocking collectives  33.9 us (17%)
  starting transfers between devices  28 us (14%)
  between operations  14.5 us (7%)
  local copies, waits for them, and re-layouts  12.2 us (6%)
  other arithmetic  5.63 us (3%)
    all_to_all x1, blocking collectives, gather_rows(): lax.all_to_all(jnp.tile(block, (count,) + (1,) * (block.ndim - 1)), axis,...  24.3 us
    psum x1, waiting for transfers between devices, body(): kernel_grad = lax.psum(kernel_part, 'fsdp')  23.7 us
    all_to_all x1, waiting for transfers between devices, table_and_gain(): got = lax.all_to_all(send, every, 0, 0, tiled=True)  21.5 us
    all_gather x1, waiting for transfers between devices, body(): lax.all_gather(kernel, 'fsdp', axis=0, tiled=True)  17.2 us
    dot_general x9, matrix products, conv_backward(): jnp.einsum('gto,goc->gtc', dpad[:, 2 * half - k:2 * half - k + length], w...  15.5 us
    dot_general x9, matrix products, conv_forward(): jnp.einsum('gtc,goc->gto', padded[:, k:k + length], weights[:, :, k * cha...  15.4 us
    all_to_all x1, waiting for transfers between devices, body(): group_in = lax.all_to_all(normed_g, 'seq', 0, 1, tiled=True)  10.3 us
    all_to_all x1, starting transfers between devices, table_and_gain(): got = lax.all_to_all(send, every, 0, 0, tiled=True)  9.92 us
  transfers between devices with their start and end apart: 9, of which 4 were waited for; matrix products, arithmetic and copies ran while one was open for 20% of the time, Pallas kernels for 0%

commit v1 on v0

--- a/solution.py
+++ b/solution.py
@@ -186,7 +186,7 @@
         scaled * mixed, axis=-1, keepdims=True
     )
     input_grad = (up_float + dmixed).astype(jnp.bfloat16)
-    kernel_grad = lax.psum(kernel_part, "fsdp")
+    kernel_grad = jnp.sum(lax.all_gather(kernel_part, "fsdp"), axis=0)
     table_grad, gain_grad = table_and_gain(input_grad, type_ids[0], gain_term, types, scale)
     return (input_grad[None], table_grad, gain_grad, kernel_grad)
 

time: 204 us -> 196 us (0.961)
  blocking collectives: 33.9 us -> 9.7 us
  waiting for transfers between devices: 73.3 us -> 90.4 us
  other arithmetic: 5.63 us -> 9.37 us
  local copies, waits for them, and re-layouts: 12.2 us -> 8.9 us
    all_to_all x1 -> x0, blocking collectives: 24.3 us -> none  [gather_rows(): lax.all_to_all(jnp.tile(block, (count,) + (1,) * (block.ndim - 1)), axis,...]
    psum x1 -> x0, waiting for transfers between devices: 23.7 us -> none  [body(): kernel_grad = lax.psum(kernel_part, 'fsdp')]
    all_to_all x0 -> x1, waiting for transfers between devices: none -> 20.3 us  [gather_rows(): lax.all_to_all(jnp.tile(block, (count,) + (1,) * (block.ndim - 1)), axis,...]
    all_to_all x1, waiting for transfers between devices: 0.01 us -> 14.8 us  [body(): group_out = lax.all_to_all(dconv, 'seq', 0, 1, tiled=True)]
    all_to_all x1, waiting for transfers between devices: 10.3 us -> 0.01 us  [body(): group_in = lax.all_to_all(normed_g, 'seq', 0, 1, tiled=True)]
    all_gather x1, waiting for transfers between devices: 17.2 us -> 27.1 us  [body(): lax.all_gather(kernel, 'fsdp', axis=0, tiled=True)]
    all_to_all x1, starting transfers between devices: 9.92 us -> 2.82 us  [table_and_gain(): got = lax.all_to_all(send, every, 0, 0, tiled=True)]
    all_to_all x1, waiting for transfers between devices: 21.5 us -> 27.5 us  [table_and_gain(): got = lax.all_to_all(send, every, 0, 0, tiled=True)]
  transfers between devices with their start and end apart: 9 -> 10, of which waited for: 4 -> 4; matrix products, arithmetic and copies ran while one was open for 20% -> 23% of each run, Pallas kernels for 0% -> 0%
where the time goes in v1:
time: 196 us; the launch traced here: 195 us
  waiting for transfers between devices  90.4 us (46%)
  matrix products  35.6 us (18%)
  starting transfers between devices  26.6 us (14%)
  between operations  14.5 us (7%)
  blocking collectives  9.7 us (5%)
  other arithmetic  9.37 us (5%)
  local copies, waits for them, and re-layouts  8.9 us (5%)
    all_to_all x1, waiting for transfers between devices, table_and_gain(): got = lax.all_to_all(send, every, 0, 0, tiled=True)  27.5 us
    all_gather x1, waiting for transfers between devices, body(): lax.all_gather(kernel, 'fsdp', axis=0, tiled=True)  27.1 us
    all_to_all x1, waiting for transfers between devices, gather_rows(): lax.all_to_all(jnp.tile(block, (count,) + (1,) * (block.ndim - 1)), axis,...  20.3 us
    dot_general x9, matrix products, conv_forward(): jnp.einsum('gtc,goc->gto', padded[:, k:k + length], weights[:, :, k * cha...  15.4 us
    all_to_all x1, waiting for transfers between devices, body(): group_out = lax.all_to_all(dconv, 'seq', 0, 1, tiled=True)  14.8 us
    dot_general x9, matrix products, conv_backward(): jnp.einsum('gto,goc->gtc', dpad[:, 2 * half - k:2 * half - k + length], w...  14.7 us
    all_to_all x1, blocking collectives, table_and_gain(): back = lax.all_to_all(back, every, 0, 0, tiled=True)  9.7 us
    ppermute x2, starting transfers between devices, with_halo(): lax.ppermute(tail, axis, [(i, (i + 1) % count) for i in range(ends)])  5.72 us
  transfers between devices with their start and end apart: 10, of which 4 were waited for; matrix products, arithmetic and copies ran while one was open for 23% of the time, Pallas kernels for 0%

profile of v1, /device:TPU:0, one launch (start us, length us, event | category | flops | bytes accessed | tf_op | source)
XLA Modules:
  0.0 195.0 jit_solution(3387529353202595104)
XLA Ops:
  7.2 0.7 all-gather.3.cloned.1.call-update
  7.9 2.0 %tile.2 = bf16[4,64,2048]{2,1,0:T(8,128)(2,1)} broadcast(bf16[64,2048]{1,0:T(8,128)(2,1)} %param.12), dimensions={1,2} | broadcast | bytes 1310720 | tf_op jit(solution)/shard_map/tile | solution.py:34
  10.0 5.3 %all-to-all-start = ((bf16[4,64,2048]{2,1,0:T(8,128)(2,1)}), bf16[4,64,2048]{2,1,0:T(8,128)(2,1)S(1)}, u32[]{:S(2)}, u32[]{:S(2)}) async-start(bf16[4,64,2048]{2,1,0:T(8,128)(2,1)} %tile.2), calls=%async_computation | async-start | bytes 2097152 | tf_op jit(solution)/shard_map/all_to_all | solution.py:33
  15.4 0.2 copy.148
  15.6 20.3 %all-to-all-done = bf16[4,64,2048]{2,1,0:T(8,128)(2,1)S(1)} async-done(((bf16[4,64,2048]{2,1,0:T(8,128)(2,1)}), bf16[4,64,2048]{2,1,0:T(8,128)(2,1)S(1)}, u32[]{:S(2)}, u32[]{:S(2)}) %all-to-all-start) | async-done | bytes 1048608 | tf_op jit(solution)/shard_map/all_to_all | solution.py:33
  35.9 1.5 multiply_reduce_fusion.2
  37.4 1.0 bitcast_bitcast_fusion
  38.4 5.2 %all-to-all-start.4 = ((bf16[16,128,128]{2,1,0:T(8,128)(2,1)}), bf16[16,128,128]{2,1,0:T(8,128)(2,1)S(1)}, u32[]{:S(2)}, u32[]{:S(2)}) async-start(bf16[16,128,128]{2,1,0:T(8,128)(2,1)} %bitcast_bitcast_fusion), calls=%async_computation.4 | async-start | bytes 1048576 | tf_op jit(solution)/shard_map/all_to_all | solution.py:163
  43.6 0.8 fusion.148
  44.4 2.4 %collective-permute-start = (bf16[16,4,128]{2,1,0:T(4,128)(2,1)S(1)}, bf16[16,4,128]{2,1,0:T(4,128)(2,1)S(1)}, u32[]{:S(2)}, u32[]{:S(2)}) collective-permute-start(bf16[16,4,128]{2,1,0:T(4,128)(2,1)S(1)} %get-tuple-element.28), channel_id=1, source_target_pairs={{0,1},{1,2},{2,3},{3,4},{4,5},{5,6},{6,7},{8,9},{9,10},{10,11},{11... | collective-permute-start | bytes 49160 | tf_op jit(solution)/shard_map/ppermute | solution.py:17
  46.8 1.3 collective-permute-start.1
  48.1 27.1 %all-gather.3.cloned.1.call-done = bf16[2048,1152]{1,0:T(8,128)(2,1)} async-done(((bf16[512,1152]{1,0:T(8,128)(2,1)}), bf16[2048,1152]{1,0:T(8,128)(2,1)}) %all-gather.3.cloned.1.call-update) | async-done | bytes 4718608 | tf_op jit(solution)/shard_map/all_gather | solution.py:152
  75.2 1.7 fusion.92
  76.9 1.7 fusion.44
  78.6 1.5 fusion.49
  80.1 1.5 fusion.69
  81.6 1.5 fusion.41
  83.2 1.5 fusion.36
  84.7 1.5 fusion.64
  86.2 1.6 fusion.13
  87.8 2.8 %fusion.18 = bf16[16,128,128]{2,1,0:T(8,128)(2,1)} fusion(f32[128,16,128]{2,1,0:T(8,128)S(1)} %bitcast.111, f32[16,128,128]{2,1,0:T(8,128)S(1)} %fusion.64, f32[16,128,128]{2,1,0:T(8,128)S(1)} %fusion.36, f32[16,128,128]{2,1,0:T(8,128)S(1)} %fusion.41, f32[16,128,128]{2,1,0:T(8,128)S(1)} %fusion.13, bf16[16,4,128]{2,1,0:T(4,128)(2,1)S(1)} %collective-permute-done.1, ...), kind=kOutput, calls=%fused_computation.37 | convolution fusion | flops 71565312 | bytes 6832128 | tf_op jit(solution)/shard_map/gtc,goc->gto/dot_general | solution.py:42
  90.6 4.6 %all-to-all-start.3 = ((bf16[16,128,128]{2,1,0:T(8,128)(2,1)}), bf16[16,128,128]{2,1,0:T(8,128)(2,1)S(1)}, u32[]{:S(2)}, u32[]{:S(2)}) async-start(bf16[16,128,128]{2,1,0:T(8,128)(2,1)} %fusion.18), calls=%async_computation.3 | async-start | bytes 1048576 | tf_op jit(solution)/shard_map/all_to_all | solution.py:164
  95.3 0.3 copy.133
  95.6 0.2 all_to_all.49
  95.8 14.8 %all-to-all-done.3 = bf16[16,128,128]{2,1,0:T(8,128)(2,1)S(1)} async-done(((bf16[16,128,128]{2,1,0:T(8,128)(2,1)}), bf16[16,128,128]{2,1,0:T(8,128)(2,1)S(1)}, u32[]{:S(2)}, u32[]{:S(2)}) %all-to-all-start.3) | async-done | bytes 524320 | tf_op jit(solution)/shard_map/all_to_all | solution.py:164
  110.7 0.4 convolution_dynamic-update-slice_fusion.8
  111.0 0.4 convolution_dynamic-update-slice_fusion.7
  111.4 0.4 convolution_dynamic-update-slice_fusion.6
  111.7 0.4 convolution_dynamic-update-slice_fusion.5
  112.1 0.3 convolution_dynamic-update-slice_fusion.4
  112.4 0.4 convolution_dynamic-update-slice_fusion.3
  112.8 0.4 convolution_dynamic-update-slice_fusion.2
  113.1 0.4 convolution_dynamic-update-slice_fusion.1
  113.5 0.4 convolution_dynamic-update-slice_fusion
  114.0 1.4 copy.134
  115.5 0.1 copy.125
  115.6 0.8 fusion.147
  116.4 1.6 collective-permute-start.2
  118.0 1.7 fusion.90
  119.7 3.3 %collective-permute-start.3 = (bf16[16,4,128]{2,1,0:T(4,128)(2,1)S(1)}, bf16[16,4,128]{2,1,0:T(4,128)(2,1)S(1)}, u32[]{:S(2)}, u32[]{:S(2)}) collective-permute-start(bf16[16,4,128]{2,1,0:T(4,128)(2,1)S(1)} %get-tuple-element.27), channel_id=1, source_target_pairs={{0,1},{1,2},{2,3},{3,4},{4,5},{5,6},{6,7},{8,9},{9,10},{10,11},{11... | collective-permute-start | bytes 49160 | tf_op jit(solution)/shard_map/ppermute | solution.py:17
  123.0 1.7 fusion.33
  124.7 1.7 fusion.28
  126.5 1.7 fusion.59
  128.2 1.6 fusion.25
  129.8 1.6 fusion.20
  131.3 1.6 fusion.54
  132.9 1.6 fusion.7
  134.5 1.6 fusion.4
  136.0 0.3 copy.144
  136.4 0.3 multiply_reduce_fusion
  136.7 1.4 fusion.16
  138.1 0.3 copy.124
  138.5 1.3 pad_maximum_fusion
  139.8 2.8 %all-to-all-start.1 = ((bf16[32,130,64]{1,2,0:T(8,128)(2,1)}), bf16[32,130,64]{1,2,0:T(8,128)(2,1)S(1)}, u32[]{:S(2)}, u32[]{:S(2)}) async-start(bf16[32,130,64]{1,2,0:T(8,128)(2,1)} %pad_maximum_fusion), calls=%async_computation.1 | async-start | bytes 2097152 | tf_op jit(solution)/shard_map/all_to_all | solution.py:111
  142.7 27.5 %all-to-all-done.1 = bf16[32,130,64]{1,2,0:T(8,128)(2,1)S(1)} async-done(((bf16[32,130,64]{1,2,0:T(8,128)(2,1)}), bf16[32,130,64]{1,2,0:T(8,128)(2,1)S(1)}, u32[]{:S(2)}, u32[]{:S(2)}) %all-to-all-start.1) | async-done | bytes 532512 | tf_op jit(solution)/shard_map/all_to_all | solution.py:111
  170.3 0.3 copy.145
  170.8 0.9 fusion.14
  171.8 0.1 reshape.135
  171.9 9.7 %all_to_all.55 = f32[32,1,576]{2,1,0:T(1,128)S(1)} all-to-all(f32[32,1,576]{2,1,0:T(1,128)S(1)} %reshape.135), channel_id=1, replica_groups=mesh['fsdp'=4,'seq'=8] {'fsdp','seq'}, dimensions={0} | all-to-all | bytes 147456 | tf_op jit(solution)/shard_map/all_to_all | solution.py:125
  181.6 0.5 broadcast.70
  182.1 0.8 reduce.7
  183.1 0.7 reshape.123
  183.8 0.6 slice_reduce_fusion
  184.4 3.7 %reduce_sum.49 = f32[256,1152]{1,0:T(8,128)} reduce(f32[4,256,1152]{2,1,0:T(8,128)} %all-gather.5.cloned.1.call-done, f32[]{:T(128)} %constant.44.clone.1), dimensions={0}, to_apply=%region_4.5 | reduce | flops 884736 | bytes 5898244 | tf_op jit(solution)/shard_map/reduce_sum | solution.py:189
  (43 shorter events, 1.1 us)
Async XLA Ops:
  7.2 8.1 %copy-start.1 = (bf16[1,128,2048]{2,1,0:T(8,128)(2,1)S(1)}, bf16[1,128,2048]{2,1,0:T(8,128)(2,1)}, u32[]{:S(2)}) copy-start(bf16[1,128,2048]{2,1,0:T(8,128)(2,1)} %param.15) | copy-start | bytes 1572868
  7.2 28.7 %copy-start.4 = (s32[1,128]{1,0:T(1,128)S(1)}, s32[1,128]{1,0:T(1,128)}, u32[]{:S(2)}) copy-start(s32[1,128]{1,0:T(1,128)} %param.11) | copy-start | bytes 1540
  7.2 68.0 %all-gather.3.cloned.1.call-start = ((), (), s32[]{:S(2)}) async-start(), calls=%async_computation.5 | async-start | bytes 5898240 | tf_op jit(solution)/shard_map/all_gather | solution.py:152
  10.0 27.4 %copy-start.3 = (f32[2048]{0:T(1024)S(1)}, f32[2048]{0:T(1024)}, u32[]{:S(2)}) copy-start(f32[2048]{0:T(1024)} %param.13) | copy-start | bytes 24580
  10.0 25.9 %all-to-all-start = ((bf16[4,64,2048]{2,1,0:T(8,128)(2,1)}), bf16[4,64,2048]{2,1,0:T(8,128)(2,1)S(1)}, u32[]{:S(2)}, u32[]{:S(2)}) async-start(bf16[4,64,2048]{2,1,0:T(8,128)(2,1)} %tile.2), calls=%async_computation | async-start | bytes 2097152 | tf_op jit(solution)/shard_map/all_to_all | solution.py:33
  38.4 52.3 %all-to-all-start.4 = ((bf16[16,128,128]{2,1,0:T(8,128)(2,1)}), bf16[16,128,128]{2,1,0:T(8,128)(2,1)S(1)}, u32[]{:S(2)}, u32[]{:S(2)}) async-start(bf16[16,128,128]{2,1,0:T(8,128)(2,1)} %bitcast_bitcast_fusion), calls=%async_computation.4 | async-start | bytes 1048576 | tf_op jit(solution)/shard_map/all_to_all | solution.py:163
  44.4 32.5 %collective-permute-start = (bf16[16,4,128]{2,1,0:T(4,128)(2,1)S(1)}, bf16[16,4,128]{2,1,0:T(4,128)(2,1)S(1)}, u32[]{:S(2)}, u32[]{:S(2)}) collective-permute-start(bf16[16,4,128]{2,1,0:T(4,128)(2,1)S(1)} %get-tuple-element.28), channel_id=1, source_target_pairs={{0,1},{1,2},{2,3},{3,4},{4,5},{5,6},{6,7},{8,9},{9,10},{10,11},{11... | collective-permute-start | bytes 49160 | tf_op jit(solution)/shard_map/ppermute | solution.py:17
  46.8 34.8 %collective-permute-start.1 = (bf16[16,4,128]{2,1,0:T(4,128)(2,1)S(1)}, bf16[16,4,128]{2,1,0:T(4,128)(2,1)S(1)}, u32[]{:S(2)}, u32[]{:S(2)}) collective-permute-start(bf16[16,4,128]{2,1,0:T(4,128)(2,1)S(1)} %get-tuple-element.29), channel_id=1, source_target_pairs={{1,0},{2,1},{3,2},{4,3},{5,4},{6,5},{7,6},{9,8},{10,9},{11,10},{12... | collective-permute-start | bytes 49160 | tf_op jit(solution)/shard_map/ppermute | solution.py:19
  75.1 3.4 %copy-start = (bf16[2048,1152]{1,0:T(8,128)(2,1)S(1)}, bf16[2048,1152]{1,0:T(8,128)(2,1)}, u32[]{:S(2)}) copy-start(bf16[2048,1152]{1,0:T(8,128)(2,1)} %all-gather.3.cloned.1.call-done) | copy-start | bytes 14155780
  90.6 20.0 %all-to-all-start.3 = ((bf16[16,128,128]{2,1,0:T(8,128)(2,1)}), bf16[16,128,128]{2,1,0:T(8,128)(2,1)S(1)}, u32[]{:S(2)}, u32[]{:S(2)}) async-start(bf16[16,128,128]{2,1,0:T(8,128)(2,1)} %fusion.18), calls=%async_computation.3 | async-start | bytes 1048576 | tf_op jit(solution)/shard_map/all_to_all | solution.py:164
  95.2 89.1 %all-gather.5.cloned.1.call-start = ((), (), s32[]{:S(2)}) async-start(), calls=%async_computation.6 | async-start | bytes 5898240 | tf_op jit(solution)/shard_map/all_gather | solution.py:189
  113.9 14.3 %slice-start = ((s8[4718592]{0:T(1024)(128)(4,1)}), s8[524288]{0:T(1024)(128)(4,1)S(1)}, s32[]{:S(2)}) async-start(s8[4718592]{0:T(1024)(128)(4,1)} %bitcast.88), calls=%async_computation.7 | async-start | bytes 1048576
  116.4 11.8 %slice-start.1 = ((s8[4718592]{0:T(1024)(128)(4,1)}), s8[4194304]{0:T(1024)(128)(4,1)S(1)}, s32[]{:S(2)}) async-start(s8[4718592]{0:T(1024)(128)(4,1)} %bitcast.88), calls=%async_computation.8 | async-start | bytes 8388608
  116.4 6.6 %collective-permute-start.2 = (bf16[16,4,128]{2,1,0:T(4,128)(2,1)S(1)}, bf16[16,4,128]{2,1,0:T(4,128)(2,1)S(1)}, u32[]{:S(2)}, u32[]{:S(2)}) collective-permute-start(bf16[16,4,128]{2,1,0:T(4,128)(2,1)S(1)} %get-tuple-element.26), channel_id=1, source_target_pairs={{1,0},{2,1},{3,2},{4,3},{5,4},{6,5},{7,6},{9,8},{10,9},{11,10},{12... | collective-permute-start | bytes 49160 | tf_op jit(solution)/shard_map/ppermute | solution.py:19
  119.7 8.5 %collective-permute-start.3 = (bf16[16,4,128]{2,1,0:T(4,128)(2,1)S(1)}, bf16[16,4,128]{2,1,0:T(4,128)(2,1)S(1)}, u32[]{:S(2)}, u32[]{:S(2)}) collective-permute-start(bf16[16,4,128]{2,1,0:T(4,128)(2,1)S(1)} %get-tuple-element.27), channel_id=1, source_target_pairs={{0,1},{1,2},{2,3},{3,4},{4,5},{5,6},{6,7},{8,9},{9,10},{10,11},{11... | collective-permute-start | bytes 49160 | tf_op jit(solution)/shard_map/ppermute | solution.py:17
  138.1 33.5 %copy-start.2 = (bf16[128,2048]{1,0:T(8,128)(2,1)}, bf16[128,2048]{1,0:T(8,128)(2,1)S(1)}, u32[]{:S(2)}) copy-start(bf16[128,2048]{1,0:T(8,128)(2,1)S(1)} %fusion.16) | copy-start | bytes 1572868
  139.8 30.4 %all-to-all-start.1 = ((bf16[32,130,64]{1,2,0:T(8,128)(2,1)}), bf16[32,130,64]{1,2,0:T(8,128)(2,1)S(1)}, u32[]{:S(2)}, u32[]{:S(2)}) async-start(bf16[32,130,64]{1,2,0:T(8,128)(2,1)} %pad_maximum_fusion), calls=%async_computation.1 | async-start | bytes 2097152 | tf_op jit(solution)/shard_map/all_to_all | solution.py:111
Sparse Core Ops, SparseCore 0:
  9.9 65.2 all-gather.2
  115.5 67.0 all-gather.4
